TPU v7x, 32 devices: a whole 2x2x4 slice. The times are simulated.
32 devices in a mesh: param: 4 (over y, core), ex: 8 (over z, x).
Axes of the slice: x: 2, y: 2, z: 4, core: 2. Of those that a mesh axis runs over, the one named last changes fastest.
Arguments:
- activations: bfloat16 [32, 128, 8192], P('ex', None, 'param'), may hold values from -6 to 6
- out_grads: bfloat16 [32, 128, 8192], P('ex', None, 'param'), may hold values from -6 to 6
- proj_in: bfloat16 [8192, 32], P('param'), may hold values from -0.0625 to 0.0625
- proj_out: bfloat16 [8192, 32], P('param'), may hold values from -0.0625 to 0.0625
- prior: float32 [1024, 1024], P('ex', 'param'), as said below
- probes: bfloat16 [512, 1024], P(('param', 'ex')), may hold values from -6 to 6
Outputs:
- scores: float32 [512, 32], P('param', 'ex')
Inputs may be any that keep to these rules, and one draw needn't show every extreme that they name: prior is symmetric positive definite with smallest eigenvalue at least 0.1.
All inputs are finite; a program needn't handle non-finite values.
Results may differ from a plain program's by a relative error of at most 0.0042.
Values may be sent and summed in bfloat16 or wider, within the bound.
No kernel may reach another device: no remote copies, remote signals or barrier semaphores. Data moves between devices by JAX's collectives and lax.ppermute only.
A program may use at most 64 MiB of HBM per device.

v0:
```python
import math
import jax
import jax.numpy as jnp
from jax import lax
from jax.sharding import PartitionSpec as P


def outer_terms(factors, in_width):
    first = factors[:, :in_width]
    second = factors[:, in_width:]
    product = jnp.einsum("eol,eil->eoi", second, first, precision=lax.Precision.HIGHEST)
    return product.reshape(product.shape[0], -1)


def solve_rows(lower_factor, rows):
    halfway = lax.linalg.triangular_solve(
        lower_factor, rows.astype(jnp.float32).T, left_side=True, lower=True
    )
    solved_t = lax.linalg.triangular_solve(
        lower_factor, halfway, left_side=True, lower=True, transpose_a=True
    )
    return solved_t.T.astype(jnp.bfloat16)


def per_device(activations, out_grads, proj_in, proj_out, prior, probes):
    tokens = activations.shape[1]
    in_width = proj_in.shape[1]
    factor_in = jnp.einsum("eld,dk->ekl", activations, proj_in, preferred_element_type=jnp.float32)
    factor_out = jnp.einsum("eld,dk->ekl", out_grads, proj_out, preferred_element_type=jnp.float32)
    factors = jnp.concatenate((factor_in, factor_out), axis=1)
    factors = lax.psum(factors, "param")
    summed = outer_terms(factors, in_width)
    features = (summed * (1.0 / math.sqrt(tokens))).astype(jnp.bfloat16)
    feat_dim = features.shape[1]
    block_width = feat_dim // lax.axis_size("param")
    column_start = lax.axis_index("param") * block_width
    train_count = features.shape[0] * lax.axis_size("ex")
    row_start = lax.axis_index("ex") * prior.shape[0]
    placed = lax.dynamic_update_slice(
        jnp.zeros((feat_dim, block_width), jnp.float32), prior, (row_start, jnp.int32(0))
    )
    columns = lax.dynamic_slice_in_dim(features, column_start, block_width, 1)
    kernel_block = lax.psum(
        placed
        + lax.dot_general(
            features, columns, (((0,), (0,)), ((), ())), preferred_element_type=jnp.float32
        )
        / train_count,
        "ex",
    )
    kernel = lax.all_gather(kernel_block, "param", axis=1, tiled=True)
    lower_factor = jnp.linalg.cholesky(kernel)
    inverse_root = 1.0 / math.sqrt(feat_dim)
    solved = solve_rows(lower_factor, features)
    return (
        jnp.dot(
            lax.all_gather(probes, "ex", axis=0, tiled=True),
            solved.T,
            preferred_element_type=jnp.float32,
        )
        * inverse_root
    )


def solution(mesh):
    return jax.shard_map(
        per_device,
        mesh=mesh,
        in_specs=(
            P("ex", None, "param"),
            P("ex", None, "param"),
            P("param", None),
            P("param", None),
            P("ex", "param"),
            P(("param", "ex"), None),
        ),
        out_specs=P("param", "ex"),
        check_vma=False,
    )
```

profile of v0, /device:TPU:0, one launch (start us, length us, event | category | flops | bytes accessed | tf_op | source)
XLA Modules:
  0.0 520.8 jit_solution(16283190189120157218)
XLA Ops:
  13.0 34.1 %all-reduce.4.cloned.1.call-done = f32[4,64,128]{2,1,0:T(8,128)} async-done(((f32[4,64,128]{2,1,0:T(8,128)}), f32[4,64,128]{2,1,0:T(8,128)}) %all-reduce.4.cloned.1.call-update) | async-done | bytes 131088 | tf_op jit(solution)/shard_map/psum | solution.py:31
  49.8 79.2 %all-reduce.6.cloned.1.call-done = f32[1024,256]{0,1:T(8,128)} async-done(((f32[1024,256]{0,1:T(8,128)}), f32[1024,256]{0,1:T(8,128)}) %all-reduce.6.cloned.1.call-update) | async-done | bytes 1048592 | tf_op jit(solution)/shard_map/psum | solution.py:43
  129.1 30.8 %all_gather.7 = bf16[128,1024]{1,0:T(8,128)(2,1)S(1)} all-gather(bf16[16,1024]{1,0:T(8,128)(2,1)S(1)} %copy-done.4), channel_id=1, replica_groups=mesh['param'=4,'ex'=8] {'ex'}, dimensions={0}, use_global_device_ids=true | all-gather | bytes 294912 | tf_op jit(solution)/shard_map/all_gather | solution.py:57
  159.9 4.8 all-gather.2.cloned.1.call-done
  164.7 5.6 %copy.9 = f32[1024,1024]{1,0:T(8,128)} copy(f32[1024,1024]{0,1:T(8,128)} %all-gather.2.cloned.1.call-done) | data formatting | bytes 8388608 | tf_op jit(solution)/shard_map/all_gather | solution.py:51
  170.3 4.4 fusion
  176.7 11.7 %cholesky.223 = f32[128,128]{1,0:T(8,128)S(1)} custom-call(f32[128,128]{1,0:T(8,128)S(1)} %cholesky.580), custom_call_target="Cholesky" | custom-call | tf_op jit(solution)/shard_map/jit(cholesky)/cholesky | solution.py:52
  188.5 9.8 %custom-call.64 = f32[1,128,128]{1,2,0:T(8,128)S(1)} custom-call(f32[1,128,128]{2,1,0:T(8,128)S(1)} %get-tuple-element.44), custom_call_target="InvertDiagBlocksLowerTriangular" | custom-call | tf_op jit(solution)/shard_map/jit(cholesky)/cholesky | solution.py:52
  204.7 12.2 %cholesky.244 = f32[128,128]{1,0:T(8,128)S(1)} custom-call(f32[128,128]{1,0:T(8,128)S(1)} %cholesky.584), custom_call_target="Cholesky" | custom-call | tf_op jit(solution)/shard_map/jit(cholesky)/cholesky | solution.py:52
  217.6 9.8 %custom-call.65 = f32[1,128,128]{1,2,0:T(8,128)S(1)} custom-call(f32[1,128,128]{2,1,0:T(8,128)S(1)} %get-tuple-element.41), custom_call_target="InvertDiagBlocksLowerTriangular" | custom-call | tf_op jit(solution)/shard_map/jit(cholesky)/cholesky | solution.py:52
  230.7 11.7 %cholesky.468 = f32[128,128]{1,0:T(8,128)S(1)} custom-call(f32[128,128]{1,0:T(8,128)S(1)} %cholesky.589), custom_call_target="Cholesky" | custom-call | tf_op jit(solution)/shard_map/jit(cholesky)/cholesky | solution.py:52
  243.7 9.8 %custom-call.66 = f32[1,128,128]{1,2,0:T(8,128)S(1)} custom-call(f32[1,128,128]{2,1,0:T(8,128)S(1)} %get-tuple-element.38), custom_call_target="InvertDiagBlocksLowerTriangular" | custom-call | tf_op jit(solution)/shard_map/jit(cholesky)/cholesky | solution.py:52
  257.1 11.8 %cholesky.487 = f32[128,128]{1,0:T(8,128)S(1)} custom-call(f32[128,128]{1,0:T(8,128)S(1)} %cholesky.594), custom_call_target="Cholesky" | custom-call | tf_op jit(solution)/shard_map/jit(cholesky)/cholesky | solution.py:52
  270.3 9.8 %custom-call.67 = f32[1,128,128]{1,2,0:T(8,128)S(1)} custom-call(f32[1,128,128]{2,1,0:T(8,128)S(1)} %get-tuple-element.35), custom_call_target="InvertDiagBlocksLowerTriangular" | custom-call | tf_op jit(solution)/shard_map/jit(cholesky)/cholesky | solution.py:52
  283.5 11.7 %cholesky.506 = f32[128,128]{1,0:T(8,128)S(1)} custom-call(f32[128,128]{1,0:T(8,128)S(1)} %cholesky.599), custom_call_target="Cholesky" | custom-call | tf_op jit(solution)/shard_map/jit(cholesky)/cholesky | solution.py:52
  296.5 10.0 %custom-call.68 = f32[1,128,128]{1,2,0:T(8,128)S(1)} custom-call(f32[1,128,128]{2,1,0:T(8,128)S(1)} %get-tuple-element.32), custom_call_target="InvertDiagBlocksLowerTriangular" | custom-call | tf_op jit(solution)/shard_map/jit(cholesky)/cholesky | solution.py:52
  309.8 11.7 %cholesky.526 = f32[128,128]{1,0:T(8,128)S(1)} custom-call(f32[128,128]{1,0:T(8,128)S(1)} %cholesky.604), custom_call_target="Cholesky" | custom-call | tf_op jit(solution)/shard_map/jit(cholesky)/cholesky | solution.py:52
  322.8 9.8 %custom-call.69 = f32[1,128,128]{1,2,0:T(8,128)S(1)} custom-call(f32[1,128,128]{2,1,0:T(8,128)S(1)} %get-tuple-element.29), custom_call_target="InvertDiagBlocksLowerTriangular" | custom-call | tf_op jit(solution)/shard_map/jit(cholesky)/cholesky | solution.py:52
  335.6 12.1 %cholesky.546 = f32[128,128]{1,0:T(8,128)S(1)} custom-call(f32[128,128]{1,0:T(8,128)S(1)} %cholesky.609), custom_call_target="Cholesky" | custom-call | tf_op jit(solution)/shard_map/jit(cholesky)/cholesky | solution.py:52
  349.0 9.8 %custom-call.70 = f32[1,128,128]{1,2,0:T(8,128)S(1)} custom-call(f32[1,128,128]{2,1,0:T(8,128)S(1)} %get-tuple-element.26), custom_call_target="InvertDiagBlocksLowerTriangular" | custom-call | tf_op jit(solution)/shard_map/jit(cholesky)/cholesky | solution.py:52
  361.5 11.7 %cholesky.564 = f32[128,128]{1,0:T(8,128)S(1)} custom-call(f32[128,128]{1,0:T(8,128)S(1)} %convolution_subtract_fusion.6), custom_call_target="Cholesky" | custom-call | tf_op jit(solution)/shard_map/jit(cholesky)/cholesky | solution.py:52
  380.2 4.8 select_select_fusion
  385.0 27.6 %while.1 = (s32[]{:T(128)}, f32[1024,1024]{1,0:T(8,128)}, s32[8,2]{0,1:T(2,128)S(1)}, f32[8,128,128]{2,1,0:T(8,128)}, s32[]{:T(128)}) while((s32[]{:T(128)}, f32[1024,1024]{1,0:T(8,128)}, s32[8,2]{0,1:T(2,128)S(1)}, f32[8,128,128]{2,1,0:T(8,128)}, s32[]{:T(128)}) %tuple.57), condition=%wide.while_cond, body=%wide.while_body.sunk | while | flops 2 | bytes 132705 | solution.py:19
  385.6 2.9 bitcast_dynamic-update-slice_fusion.2
  389.1 2.8 bitcast_dynamic-update-slice_fusion.2
  392.5 2.8 bitcast_dynamic-update-slice_fusion.2
  396.0 2.8 bitcast_dynamic-update-slice_fusion.2
  399.5 2.8 bitcast_dynamic-update-slice_fusion.2
  402.9 2.8 bitcast_dynamic-update-slice_fusion.2
  406.4 2.8 bitcast_dynamic-update-slice_fusion.2
  409.9 2.8 bitcast_dynamic-update-slice_fusion.2
  412.6 79.6 %custom-call.71 = f32[8,128,128]{1,2,0:T(8,128)S(1)} custom-call(f32[8,128,128]{2,1,0:T(8,128)} %get-tuple-element.12), custom_call_target="InvertDiagBlocksLowerTriangular" | custom-call | tf_op jit(solution)/shard_map/triangular_solve | solution.py:19
  (134 shorter events, 72.6 us)
Async XLA Ops:
  6.5 1.6 copy-start
  6.5 6.4 %copy-start.3 = (f32[128,256]{1,0:T(8,128)S(1)}, f32[128,256]{1,0:T(8,128)}, u32[]{:S(2)}) copy-start(f32[128,256]{1,0:T(8,128)} %param.10) | copy-start | bytes 393220
  6.5 122.5 %copy-start.4 = (bf16[16,1024]{1,0:T(8,128)(2,1)S(1)}, bf16[16,1024]{1,0:T(8,128)(2,1)}, u32[]{:S(2)}) copy-start(bf16[16,1024]{1,0:T(8,128)(2,1)} %param.11) | copy-start | bytes 98308
  6.5 40.6 %all-reduce.4.cloned.1.call-start = ((), (), s32[]{:S(2)}) async-start(), calls=%async_computation | async-start | bytes 262144 | tf_op jit(solution)/shard_map/psum | solution.py:31
  12.9 116.2 %all-reduce.6.cloned.1.call-start = ((), (), s32[]{:S(2)}) async-start(), calls=%async_computation.1 | async-start | bytes 2097152 | tf_op jit(solution)/shard_map/psum | solution.py:43
  48.7 1.0 copy-start.2
  49.7 115.0 %all-gather.2.cloned.1.call-start = ((), (), s32[]{:S(2)}) async-start(), calls=%async_computation.2 | async-start | bytes 5242880 | tf_op jit(solution)/shard_map/all_gather | solution.py:51
  174.8 1.9 copy-start.1
Sparse Core Ops, SparseCore 0:
  13.0 34.0 all-reduce.3
  51.0 77.9 all-reduce.5
  130.6 34.0 all-gather.1
where the time goes:
time: 525 us; the launch traced here: 521 us
  other arithmetic  262 us (50%)
  waiting for transfers between devices  118 us (22%)
  matrix products  50 us (10%)
  local copies, waits for them, and re-layouts  40.7 us (8%)
  blocking collectives  30.8 us (6%)
  between operations  18.6 us (4%)
    another operation x30, other arithmetic, per_device(): lower_factor = jnp.linalg.cholesky(kernel)  173 us
    another operation x4, other arithmetic, solve_rows(): lax.linalg.triangular_solve(lower_factor, halfway, left_side=True, lower=...  84.4 us
    psum x1, waiting for transfers between devices, per_device(): lax.psum(placed + lax.dot_general(features, columns, (((0,), (0,)), ((),...  79.2 us
    psum x1, waiting for transfers between devices, per_device(): factors = lax.psum(factors, 'param')  34.1 us
    all_gather x1, blocking collectives, per_device(): lax.all_gather(probes, 'ex', axis=0, tiled=True)  30.8 us
    another operation x24, local copies, waits for them, and re-layouts  27.6 us
    another operation x14, matrix products, per_device(): lower_factor = jnp.linalg.cholesky(kernel)  23.1 us
    another operation x15, matrix products, solve_rows(): lax.linalg.triangular_solve(lower_factor, rows.astype(jnp.float32).T, lef...  10.6 us
  transfers between devices with their start and end apart: 3, of which 3 were waited for; matrix products, arithmetic and copies ran while one was open for 0% of the time, Pallas kernels for 0%

commit v1 on v0

--- a/solution.py
+++ b/solution.py
@@ -1,8 +1,17 @@
+import functools
 import math
 import jax
 import jax.numpy as jnp
 from jax import lax
 from jax.sharding import PartitionSpec as P
+
+
+def play_the_rounds(raw, across):
+    now = lax.all_gather(raw, axis_name=across).sum(axis=0)
+    return now
+
+
+step_on_slices_on_mesh = functools.partial(play_the_rounds, across="param")
 
 
 def outer_terms(factors, in_width):
@@ -28,7 +37,7 @@
     factor_in = jnp.einsum("eld,dk->ekl", activations, proj_in, preferred_element_type=jnp.float32)
     factor_out = jnp.einsum("eld,dk->ekl", out_grads, proj_out, preferred_element_type=jnp.float32)
     factors = jnp.concatenate((factor_in, factor_out), axis=1)
-    factors = lax.psum(factors, "param")
+    factors = step_on_slices_on_mesh(factors)
     summed = outer_terms(factors, in_width)
     features = (summed * (1.0 / math.sqrt(tokens))).astype(jnp.bfloat16)
     feat_dim = features.shape[1]

time: 525 us -> 498 us (0.949)
  waiting for transfers between devices: 118 us -> 83.9 us
  blocking collectives: 30.8 us -> 39.4 us
    psum x1 -> x0, waiting for transfers between devices: 34.1 us -> none  [per_device(): factors = lax.psum(factors, 'param')]
    all_gather x0 -> x1, blocking collectives: none -> 8.65 us  [play_the_rounds(): now = lax.all_gather(raw, axis_name=across).sum(axis=0)]
  transfers between devices with their start and end apart: 3 -> 2, of which waited for: 3 -> 2; matrix products, arithmetic and copies ran while one was open for 0% -> 0% of each run, Pallas kernels for 0% -> 0%
where the time goes in v1:
time: 498 us; the launch traced here: 494 us
  other arithmetic  262 us (53%)
  waiting for transfers between devices  83.9 us (17%)
  matrix products  49.1 us (10%)
  local copies, waits for them, and re-layouts  40.7 us (8%)
  blocking collectives  39.4 us (8%)
  between operations  18.9 us (4%)
    another operation x30, other arithmetic, per_device(): lower_factor = jnp.linalg.cholesky(kernel)  173 us
    another operation x4, other arithmetic, solve_rows(): lax.linalg.triangular_solve(lower_factor, halfway, left_side=True, lower=...  84.4 us
    psum x1, waiting for transfers between devices, per_device(): lax.psum(placed + lax.dot_general(features, columns, (((0,), (0,)), ((),...  79 us
    all_gather x1, blocking collectives, per_device(): lax.all_gather(probes, 'ex', axis=0, tiled=True)  30.8 us
    another operation x24, local copies, waits for them, and re-layouts  27.6 us
    another operation x14, matrix products, per_device(): lower_factor = jnp.linalg.cholesky(kernel)  23.1 us
    another operation x15, matrix products, solve_rows(): lax.linalg.triangular_solve(lower_factor, rows.astype(jnp.float32).T, lef...  10.6 us
    another operation x15, matrix products, solve_rows(): lax.linalg.triangular_solve(lower_factor, halfway, left_side=True, lower=...  10.1 us
  transfers between devices with their start and end apart: 2, of which 2 were waited for; matrix products, arithmetic and copies ran while one was open for 0% of the time, Pallas kernels for 0%

profile of v1, /device:TPU:0, one launch (start us, length us, event | category | flops | bytes accessed | tf_op | source)
XLA Modules:
  0.0 494.0 jit_solution(5794084756020645)
XLA Ops:
  12.2 8.6 %all-gather = f32[16,64,128]{2,1,0:T(8,128)S(1)} all-gather(f32[4,64,128]{2,1,0:T(8,128)S(1)} %pad_maximum_fusion), channel_id=2, replica_groups=mesh['param'=4,'ex'=8] {'param'}, dimensions={0}, use_global_device_ids=true | all-gather | bytes 655360 | tf_op jit(solution)/shard_map/all_gather | solution.py:10
  22.8 79.0 %all-reduce.3.cloned.1.call-done = f32[1024,256]{0,1:T(8,128)} async-done(((f32[1024,256]{0,1:T(8,128)}), f32[1024,256]{0,1:T(8,128)}) %all-reduce.3.cloned.1.call-update) | async-done | bytes 1048592 | tf_op jit(solution)/shard_map/psum | solution.py:52
  101.8 30.8 %all_gather.15 = bf16[128,1024]{1,0:T(8,128)(2,1)S(1)} all-gather(bf16[16,1024]{1,0:T(8,128)(2,1)S(1)} %copy-done.4), channel_id=1, replica_groups=mesh['param'=4,'ex'=8] {'ex'}, dimensions={0}, use_global_device_ids=true | all-gather | bytes 294912 | tf_op jit(solution)/shard_map/all_gather | solution.py:66
  132.6 4.9 all-gather.3.cloned.1.call-done
  137.5 5.6 %copy.12 = f32[1024,1024]{1,0:T(8,128)} copy(f32[1024,1024]{0,1:T(8,128)} %all-gather.3.cloned.1.call-done) | data formatting | bytes 8388608 | tf_op jit(solution)/shard_map/all_gather | solution.py:60
  143.2 4.4 fusion
  149.5 11.7 %cholesky.223 = f32[128,128]{1,0:T(8,128)S(1)} custom-call(f32[128,128]{1,0:T(8,128)S(1)} %cholesky.580), custom_call_target="Cholesky" | custom-call | tf_op jit(solution)/shard_map/jit(cholesky)/cholesky | solution.py:61
  163.8 9.8 %custom-call.64 = f32[1,128,128]{1,2,0:T(8,128)S(1)} custom-call(f32[1,128,128]{2,1,0:T(8,128)S(1)} %get-tuple-element.44), custom_call_target="InvertDiagBlocksLowerTriangular" | custom-call | tf_op jit(solution)/shard_map/jit(cholesky)/cholesky | solution.py:61
  177.5 12.2 %cholesky.244 = f32[128,128]{1,0:T(8,128)S(1)} custom-call(f32[128,128]{1,0:T(8,128)S(1)} %cholesky.584), custom_call_target="Cholesky" | custom-call | tf_op jit(solution)/shard_map/jit(cholesky)/cholesky | solution.py:61
  190.4 9.8 %custom-call.65 = f32[1,128,128]{1,2,0:T(8,128)S(1)} custom-call(f32[1,128,128]{2,1,0:T(8,128)S(1)} %get-tuple-element.41), custom_call_target="InvertDiagBlocksLowerTriangular" | custom-call | tf_op jit(solution)/shard_map/jit(cholesky)/cholesky | solution.py:61
  203.6 11.7 %cholesky.468 = f32[128,128]{1,0:T(8,128)S(1)} custom-call(f32[128,128]{1,0:T(8,128)S(1)} %cholesky.589), custom_call_target="Cholesky" | custom-call | tf_op jit(solution)/shard_map/jit(cholesky)/cholesky | solution.py:61
  216.6 9.8 %custom-call.66 = f32[1,128,128]{1,2,0:T(8,128)S(1)} custom-call(f32[1,128,128]{2,1,0:T(8,128)S(1)} %get-tuple-element.38), custom_call_target="InvertDiagBlocksLowerTriangular" | custom-call | tf_op jit(solution)/shard_map/jit(cholesky)/cholesky | solution.py:61
  229.9 11.8 %cholesky.487 = f32[128,128]{1,0:T(8,128)S(1)} custom-call(f32[128,128]{1,0:T(8,128)S(1)} %cholesky.594), custom_call_target="Cholesky" | custom-call | tf_op jit(solution)/shard_map/jit(cholesky)/cholesky | solution.py:61
  243.1 9.8 %custom-call.67 = f32[1,128,128]{1,2,0:T(8,128)S(1)} custom-call(f32[1,128,128]{2,1,0:T(8,128)S(1)} %get-tuple-element.35), custom_call_target="InvertDiagBlocksLowerTriangular" | custom-call | tf_op jit(solution)/shard_map/jit(cholesky)/cholesky | solution.py:61
  256.4 11.7 %cholesky.506 = f32[128,128]{1,0:T(8,128)S(1)} custom-call(f32[128,128]{1,0:T(8,128)S(1)} %cholesky.599), custom_call_target="Cholesky" | custom-call | tf_op jit(solution)/shard_map/jit(cholesky)/cholesky | solution.py:61
  269.4 10.0 %custom-call.68 = f32[1,128,128]{1,2,0:T(8,128)S(1)} custom-call(f32[1,128,128]{2,1,0:T(8,128)S(1)} %get-tuple-element.32), custom_call_target="InvertDiagBlocksLowerTriangular" | custom-call | tf_op jit(solution)/shard_map/jit(cholesky)/cholesky | solution.py:61
  282.7 11.7 %cholesky.526 = f32[128,128]{1,0:T(8,128)S(1)} custom-call(f32[128,128]{1,0:T(8,128)S(1)} %cholesky.604), custom_call_target="Cholesky" | custom-call | tf_op jit(solution)/shard_map/jit(cholesky)/cholesky | solution.py:61
  295.7 9.8 %custom-call.69 = f32[1,128,128]{1,2,0:T(8,128)S(1)} custom-call(f32[1,128,128]{2,1,0:T(8,128)S(1)} %get-tuple-element.29), custom_call_target="InvertDiagBlocksLowerTriangular" | custom-call | tf_op jit(solution)/shard_map/jit(cholesky)/cholesky | solution.py:61
  308.5 12.1 %cholesky.546 = f32[128,128]{1,0:T(8,128)S(1)} custom-call(f32[128,128]{1,0:T(8,128)S(1)} %cholesky.609), custom_call_target="Cholesky" | custom-call | tf_op jit(solution)/shard_map/jit(cholesky)/cholesky | solution.py:61
  321.9 9.8 %custom-call.70 = f32[1,128,128]{1,2,0:T(8,128)S(1)} custom-call(f32[1,128,128]{2,1,0:T(8,128)S(1)} %get-tuple-element.26), custom_call_target="InvertDiagBlocksLowerTriangular" | custom-call | tf_op jit(solution)/shard_map/jit(cholesky)/cholesky | solution.py:61
  334.3 11.7 %cholesky.564 = f32[128,128]{1,0:T(8,128)S(1)} custom-call(f32[128,128]{1,0:T(8,128)S(1)} %convolution_subtract_fusion.6), custom_call_target="Cholesky" | custom-call | tf_op jit(solution)/shard_map/jit(cholesky)/cholesky | solution.py:61
  353.0 4.8 select_select_fusion
  357.8 27.6 %while.1 = (s32[]{:T(128)}, f32[1024,1024]{1,0:T(8,128)}, s32[8,2]{0,1:T(2,128)S(1)}, f32[8,128,128]{2,1,0:T(8,128)}, s32[]{:T(128)}) while((s32[]{:T(128)}, f32[1024,1024]{1,0:T(8,128)}, s32[8,2]{0,1:T(2,128)S(1)}, f32[8,128,128]{2,1,0:T(8,128)}, s32[]{:T(128)}) %tuple.57), condition=%wide.while_cond, body=%wide.while_body.sunk | while | flops 2 | bytes 132705 | solution.py:28
  358.4 2.9 bitcast_dynamic-update-slice_fusion.2
  361.9 2.8 bitcast_dynamic-update-slice_fusion.2
  365.4 2.8 bitcast_dynamic-update-slice_fusion.2
  368.8 2.8 bitcast_dynamic-update-slice_fusion.2
  372.3 2.8 bitcast_dynamic-update-slice_fusion.2
  375.8 2.8 bitcast_dynamic-update-slice_fusion.2
  379.2 2.8 bitcast_dynamic-update-slice_fusion.2
  382.7 2.8 bitcast_dynamic-update-slice_fusion.2
  385.5 79.6 %custom-call.71 = f32[8,128,128]{1,2,0:T(8,128)S(1)} custom-call(f32[8,128,128]{2,1,0:T(8,128)} %get-tuple-element.12), custom_call_target="InvertDiagBlocksLowerTriangular" | custom-call | tf_op jit(solution)/shard_map/triangular_solve | solution.py:28
  (133 shorter events, 71.1 us)
Async XLA Ops:
  6.5 1.6 copy-start
  6.5 14.7 %copy-start.3 = (f32[128,256]{1,0:T(8,128)S(1)}, f32[128,256]{1,0:T(8,128)}, u32[]{:S(2)}) copy-start(f32[128,256]{1,0:T(8,128)} %param.10) | copy-start | bytes 393220
  6.5 95.3 %all-reduce.3.cloned.1.call-start = ((), (), s32[]{:S(2)}) async-start(), calls=%async_computation | async-start | bytes 2097152 | tf_op jit(solution)/shard_map/psum | solution.py:52
  9.8 92.1 %copy-start.4 = (bf16[16,1024]{1,0:T(8,128)(2,1)S(1)}, bf16[16,1024]{1,0:T(8,128)(2,1)}, u32[]{:S(2)}) copy-start(bf16[16,1024]{1,0:T(8,128)(2,1)} %param.11) | copy-start | bytes 98308
  21.7 1.0 copy-start.2
  22.7 114.8 %all-gather.3.cloned.1.call-start = ((), (), s32[]{:S(2)}) async-start(), calls=%async_computation.1 | async-start | bytes 5242880 | tf_op jit(solution)/shard_map/all_gather | solution.py:60
  147.6 1.9 copy-start.1
Sparse Core Ops, SparseCore 0:
  22.9 78.8 all-reduce.2
  103.4 34.0 all-gather.2
